TPU v7x, 256 devices: a whole 4x4x8 slice. The times are simulated.
256 devices in a mesh: pair: 128 (over x, z, y), aux: 2 (over core).
Axes of the slice: x: 4, y: 4, z: 8, core: 2. Of those that a mesh axis runs over, the one named last changes fastest.
Arguments:
- amplitudes: bfloat16 [16384, 128, 128], P('pair', 'aux'), may hold values from -6 to 6
- k_term: bfloat16 [16384, 128, 128], P('pair', 'aux'), may hold values from -6 to 6
- margin_table: bfloat16 [1024, 128, 128], P('pair'), may hold values from -0.5 to 0.5
- margin_index: int32 [16384], P('pair'), may hold values from 0 to 7
- factors: bfloat16 [128, 512, 128], P('pair', 'aux'), may hold values from -6 to 6
- vir_energy: float32 [16384, 128], P('pair'), may hold values from 0.5 to 3
- occ_energy: float32 [128], replicated, may hold values from -2 to -0.3
- pair_owner: int32 [16384, 1], P('pair'), may hold values from 0 to 127; in each aligned block of 128 rows (0 to 127, 128 to 255, ...) at most 2 rows name the same one
Outputs:
- updated: bfloat16 [16384, 128, 128], P('pair', 'aux')
Inputs may be any that keep to these rules, and one draw needn't show every extreme that they name: `pair_owner`: no more than 2 of the 128 pairs of one aligned block name the same owner. `margin_index`: an index into the 8 margin blocks that belong to the pair's aligned block of 128 pairs.
All inputs are finite; a program needn't handle non-finite values.
Results may differ from a plain program's by a relative error of at most 0.0055.
Values may be sent and summed in bfloat16 or wider, within the bound.
No kernel may reach another device: no remote copies, remote signals or barrier semaphores. Data moves between devices by JAX's collectives and lax.ppermute only.
A program may use at most 128 MiB of HBM per device.

v0:
```python
import jax
import jax.numpy as jnp
from jax import lax
from jax.sharding import PartitionSpec as P


def local(
    amplitudes, k_term, margin_table, margin_index, factors, vir_energy, occ_energy, pair_owner
):
    axis_pairs = lax.axis_size("pair")
    aux_count = lax.axis_size("aux")
    own_index = lax.axis_index("pair")
    aux_index = lax.axis_index("aux")
    pair_count = amplitudes.shape[0]
    row_count = amplitudes.shape[1]
    vir_width = amplitudes.shape[2]
    aux_rows = factors.shape[1]
    ovl_count = margin_table.shape[0]
    cycle_scale = float(vir_width * aux_rows * aux_count * pair_count) ** (-0.5)
    every_factor = lax.all_gather(factors[0], ("pair", "aux"), axis=0, tiled=True)
    every_factor = every_factor.reshape(axis_pairs, aux_count * aux_rows, vir_width)
    own_factors = lax.dynamic_index_in_dim(every_factor, own_index, 0, keepdims=False)
    full_amp = lax.all_gather(amplitudes, "aux", axis=1, tiled=True)
    block_pick = (margin_index[:, None] == jnp.arange(ovl_count, dtype=jnp.int32)[None, :]).astype(
        jnp.bfloat16
    )
    margin = jnp.einsum(
        "po,oab->pab", block_pick, margin_table, preferred_element_type=jnp.float32
    ).astype(jnp.bfloat16)
    halfway = jnp.einsum(
        "pca,pab->pcb", full_amp, margin, preferred_element_type=jnp.float32
    ).astype(jnp.bfloat16)
    rotated = jnp.einsum(
        "pac,pab->pcb", margin, halfway, preferred_element_type=jnp.float32
    ).astype(jnp.bfloat16)
    rotated = lax.dynamic_slice_in_dim(rotated, aux_index * row_count, row_count, 1)
    pair_dest = pair_owner[:, 0]
    owner_pick = (jnp.arange(axis_pairs, dtype=jnp.int32)[:, None] == pair_dest[None, :]).astype(
        jnp.bfloat16
    )
    outgoing = jnp.einsum(
        "jp,pcb->jcb", owner_pick, rotated, preferred_element_type=jnp.float32
    ).astype(jnp.bfloat16)
    incoming = lax.all_to_all(outgoing, "pair", 0, 0, tiled=True)
    dressed = jnp.einsum(
        "ica,iqa->cq", incoming, every_factor, preferred_element_type=jnp.float32
    ).astype(jnp.bfloat16)
    local_cycle = jnp.dot(dressed, own_factors, preferred_element_type=jnp.float32)
    cycle_vals = (cycle_scale * local_cycle).astype(jnp.bfloat16)
    slot_back = jnp.broadcast_to(cycle_vals[None], (axis_pairs, row_count, vir_width))
    returned = lax.all_to_all(slot_back, "pair", 0, 0, tiled=True)
    own_cycle = jnp.einsum(
        "jp,jca->pca", owner_pick, returned, preferred_element_type=jnp.float32
    ).astype(jnp.bfloat16)
    cycle_term = jnp.einsum("pca,pba->pcb", own_cycle, margin, preferred_element_type=jnp.float32)
    occ_sum = occ_energy[own_index] + occ_energy[pair_dest]
    energy_rows = lax.dynamic_slice_in_dim(vir_energy, aux_index * row_count, row_count, 1)
    denominator = energy_rows[:, :, None] + vir_energy[:, None, :] - occ_sum[:, None, None]
    updated = (
        amplitudes.astype(jnp.float32) - (cycle_term + k_term.astype(jnp.float32)) / denominator
    )
    return updated.astype(jnp.bfloat16)


def solution(mesh):
    placed = (
        P("pair", "aux", None),
        P("pair", "aux", None),
        P("pair", None, None),
        P("pair"),
        P("pair", "aux", None),
        P("pair", None),
        P(),
        P("pair", None),
    )
    return jax.shard_map(
        local, mesh=mesh, in_specs=placed, out_specs=P("pair", "aux", None), check_vma=False
    )
```

profile of v0, /device:TPU:32, one launch (start us, length us, event | category | flops | bytes accessed | tf_op | source)
XLA Modules:
  0.0 267.1 jit_solution(3907826029855658009)
XLA Ops:
  6.5 0.0 copy-start
  6.5 0.0 all-gather.4.cloned.1.call-start
  6.5 0.7 all-gather.4.cloned.1.call-update
  7.3 0.0 all-gather.6.cloned.1.call-start
  7.3 0.7 all-gather.6.cloned.1.call-update
  8.0 0.0 copy-done
  8.0 3.9 %convolution_convert_fusion = bf16[128,128,128]{2,0,1:T(8,128)(2,1)} fusion(bf16[8,128,128]{2,1,0:T(8,128)(2,1)S(1)} %copy-done, s32[128]{0:T(128)} %param.11), kind=kOutput, calls=%fused_computation.11 | convolution fusion | flops 35652608 | bytes 4456960 | tf_op jit(solution)/shard_map/po,oab->pab/dot_general | solution.py:27
  11.9 18.9 %all-gather.4.cloned.1.call-done = bf16[128,128,128]{2,1,0:T(8,128)(2,1)} async-done(((bf16[128,64,128]{2,1,0:T(8,128)(2,1)}), bf16[128,128,128]{2,1,0:T(8,128)(2,1)}) %all-gather.4.cloned.1.call-update) | async-done | bytes 4194320 | tf_op jit(solution)/shard_map/all_gather | solution.py:23
  30.8 13.0 %fusion = bf16[128,128,128]{2,1,0:T(8,128)(2,1)} fusion(bf16[128,128,128]{2,1,0:T(8,128)(2,1)} %all-gather.4.cloned.1.call-done, bf16[128,128,128]{2,0,1:T(8,128)(2,1)} %convolution_convert_fusion), kind=kOutput, calls=%fused_computation.5 | convolution fusion | flops 1075838976 | bytes 12582912 | tf_op jit(solution)/shard_map/pac,pab->pcb/dot_general | solution.py:33
  43.8 0.0 copy-start.4
  43.8 1.8 dynamic-slice_convert_fusion
  45.6 0.0 copy-done.4
  45.6 1.8 fusion.10
  47.4 2.7 %copy.36 = bf16[128,64,128]{2,1,0:T(8,128)(2,1)} copy(bf16[128,64,128]{2,0,1:T(8,128)(2,1)S(1)} %fusion.10) | data formatting | bytes 4194304 | tf_op jit(solution)/shard_map/jp,pcb->jcb/dot_general | solution.py:41
  50.0 13.7 %all-to-all-start = ((bf16[128,64,128]{2,1,0:T(8,128)(2,1)}), bf16[128,64,128]{2,1,0:T(8,128)(2,1)S(1)}, u32[]{:S(2)}, u32[]{:S(2)}) async-start(bf16[128,64,128]{2,1,0:T(8,128)(2,1)} %copy.36), calls=%async_computation | async-start | bytes 4194304 | tf_op jit(solution)/shard_map/all_to_all | solution.py:44
  63.7 59.4 %all-to-all-done = bf16[128,64,128]{2,1,0:T(8,128)(2,1)S(1)} async-done(((bf16[128,64,128]{2,1,0:T(8,128)(2,1)}), bf16[128,64,128]{2,1,0:T(8,128)(2,1)S(1)}, u32[]{:S(2)}, u32[]{:S(2)}) %all-to-all-start) | async-done | bytes 2097184 | tf_op jit(solution)/shard_map/all_to_all | solution.py:44
  123.1 43.7 %all-gather.6.cloned.1.call-done = bf16[1,65536,128]{2,1,0:T(8,128)(2,1)} async-done(((bf16[1,256,128]{2,1,0:T(8,128)(2,1)}), bf16[1,65536,128]{2,1,0:T(8,128)(2,1)}) %all-gather.6.cloned.1.call-update) | async-done | bytes 16777232 | tf_op jit(solution)/shard_map/all_gather | solution.py:20
  166.8 11.0 %fusion.15 = bf16[64,128]{1,0:T(8,128)(2,1)S(1)} fusion(bf16[128,64,128]{2,1,0:T(8,128)(2,1)S(1)} %all-to-all-done, bf16[128,512,128]{2,1,0:T(8,128)(2,1)} %bitcast.24, s32[]{:T(128)S(6)} %select_n.14), kind=kOutput, calls=%fused_computation.19 | convolution fusion | flops 1082179584 | bytes 19021828 | tf_op jit(solution)/shard_map/dot_general | solution.py:48
  177.8 0.0 copy-start.1
  177.9 0.0 copy-start.3
  177.9 1.8 broadcast_in_dim.2
  179.7 9.7 %all-to-all-start.1 = ((bf16[128,64,128]{2,1,0:T(8,128)(2,1)}), bf16[128,64,128]{2,1,0:T(8,128)(2,1)S(1)}, u32[]{:S(2)}, u32[]{:S(2)}) async-start(bf16[128,64,128]{2,1,0:T(8,128)(2,1)} %broadcast_in_dim.2), calls=%async_computation.1 | async-start | bytes 4194304 | tf_op jit(solution)/shard_map/all_to_all | solution.py:51
  189.5 0.0 copy-done.1
  189.5 0.6 dynamic_slice.16
  190.1 1.2 gather_fusion
  191.3 0.0 copy-done.3
  191.3 0.1 constant_dynamic-slice_fusion
  191.4 0.6 broadcast_add_fusion
  192.1 50.2 %all-to-all-done.1 = bf16[128,64,128]{2,1,0:T(8,128)(2,1)S(1)} async-done(((bf16[128,64,128]{2,1,0:T(8,128)(2,1)}), bf16[128,64,128]{2,1,0:T(8,128)(2,1)S(1)}, u32[]{:S(2)}, u32[]{:S(2)}) %all-to-all-start.1) | async-done | bytes 2097184 | tf_op jit(solution)/shard_map/all_to_all | solution.py:51
  242.3 0.0 copy-start.2
  242.3 1.8 fusion.8
  244.0 0.4 copy-done.2
  244.5 15.8 %subtract_convert_fusion = bf16[128,64,128]{2,1,0:T(8,128)(2,1)} fusion(bf16[128,64,128]{2,1,0:T(8,128)(2,1)} %param.9, bf16[128,64,128]{2,1,0:T(8,128)(2,1)} %param.8, f32[128]{0:T(128)S(1)} %broadcast_add_fusion, f32[128,128]{1,0:T(8,128)S(1)} %copy-done.3, f32[128,64]{1,0:T(8,128)S(1)} %constant_dynamic-slice_fusion, ...), kind=kOutput, calls=%fused_computation.4 | convolution fusion | flops 276824064 | bytes 12681728 | tf_op jit(solution)/shard_map/pca,pba->pcb/dot_general | solution.py:55
  (2 shorter events, 0.0 us)
Async XLA Ops:
  6.5 1.5 copy-start
  6.5 24.2 %all-gather.4.cloned.1.call-start = ((), (), s32[]{:S(2)}) async-start(), calls=%async_computation.2 | async-start | bytes 6291456 | tf_op jit(solution)/shard_map/all_gather | solution.py:23
  7.3 159.6 %all-gather.6.cloned.1.call-start = ((), (), s32[]{:S(2)}) async-start(), calls=%async_computation.3 | async-start | bytes 16842752 | tf_op jit(solution)/shard_map/all_gather | solution.py:20
  43.8 1.8 copy-start.4
  50.0 73.1 %all-to-all-start = ((bf16[128,64,128]{2,1,0:T(8,128)(2,1)}), bf16[128,64,128]{2,1,0:T(8,128)(2,1)S(1)}, u32[]{:S(2)}, u32[]{:S(2)}) async-start(bf16[128,64,128]{2,1,0:T(8,128)(2,1)} %copy.36), calls=%async_computation | async-start | bytes 4194304 | tf_op jit(solution)/shard_map/all_to_all | solution.py:44
  177.8 11.6 %copy-start.1 = (f32[128]{0:T(128)S(1)}, f32[128]{0:T(128)}, u32[]{:S(2)}) copy-start(f32[128]{0:T(128)} %param.14) | copy-start | bytes 1540
  177.9 13.5 %copy-start.3 = (f32[128,128]{1,0:T(8,128)S(1)}, f32[128,128]{1,0:T(8,128)}, u32[]{:S(2)}) copy-start(f32[128,128]{1,0:T(8,128)} %param.13) | copy-start | bytes 196612
  179.7 62.6 %all-to-all-start.1 = ((bf16[128,64,128]{2,1,0:T(8,128)(2,1)}), bf16[128,64,128]{2,1,0:T(8,128)(2,1)S(1)}, u32[]{:S(2)}, u32[]{:S(2)}) async-start(bf16[128,64,128]{2,1,0:T(8,128)(2,1)} %broadcast_in_dim.2), calls=%async_computation.1 | async-start | bytes 4194304 | tf_op jit(solution)/shard_map/all_to_all | solution.py:51
  242.3 2.2 copy-start.2
Sparse Core Ops, SparseCore 0:
  9.1 21.6 all-gather.3
  34.5 132.2 all-gather.5
where the time goes:
time: 267 us
  waiting for transfers between devices  174 us (65%)
  matrix products  47.2 us (18%)
  starting transfers between devices  23.5 us (9%)
  between operations  13.5 us (5%)
  local copies, waits for them, and re-layouts  8.68 us (3%)
    all_to_all x1, waiting for transfers between devices, local(): incoming = lax.all_to_all(outgoing, 'pair', 0, 0, tiled=True)  59.4 us
    all_to_all x1, waiting for transfers between devices, local(): returned = lax.all_to_all(slot_back, 'pair', 0, 0, tiled=True)  50.2 us
    all_gather x1, waiting for transfers between devices, local(): lax.all_gather(factors[0], ('pair', 'aux'), axis=0, tiled=True)  43.7 us
    all_gather x1, waiting for transfers between devices, local(): full_amp = lax.all_gather(amplitudes, 'aux', axis=1, tiled=True)  18.9 us
    dot_general x1, matrix products, local(): jnp.einsum('pca,pba->pcb', own_cycle, margin, preferred_element_type=jnp....  15.8 us
    all_to_all x1, starting transfers between devices, local(): incoming = lax.all_to_all(outgoing, 'pair', 0, 0, tiled=True)  13.7 us
    dot_general x1, matrix products, local(): jnp.einsum('pac,pab->pcb', margin, halfway, preferred_element_type=jnp.fl...  13 us
    dot_general x1, matrix products, local(): jnp.dot(dressed, own_factors, preferred_element_type=jnp.float32)  11 us
  transfers between devices with their start and end apart: 4, of which 4 were waited for; matrix products, arithmetic and copies ran while one was open for 10% of the time, Pallas kernels for 0%

commit v1 on v0

--- a/solution.py
+++ b/solution.py
@@ -20,7 +20,10 @@
     every_factor = lax.all_gather(factors[0], ("pair", "aux"), axis=0, tiled=True)
     every_factor = every_factor.reshape(axis_pairs, aux_count * aux_rows, vir_width)
     own_factors = lax.dynamic_index_in_dim(every_factor, own_index, 0, keepdims=False)
-    full_amp = lax.all_gather(amplitudes, "aux", axis=1, tiled=True)
+    devices = lax.axis_size("aux")
+    shards = jnp.stack([amplitudes for _ in range(devices)])
+    shards = lax.all_to_all(shards, "aux", split_axis=0, concat_axis=0)
+    full_amp = jnp.concatenate(shards, axis=1)
     block_pick = (margin_index[:, None] == jnp.arange(ovl_count, dtype=jnp.int32)[None, :]).astype(
         jnp.bfloat16
     )

time: 267 us -> 252 us (0.944)
  waiting for transfers between devices: 174 us -> 138 us
  starting transfers between devices: 23.5 us -> 32.4 us
  local copies, waits for them, and re-layouts: 8.68 us -> 14.4 us
  other arithmetic: 0.65 us -> 5.23 us
    all_gather x1, waiting for transfers between devices: 43.7 us -> 18.1 us  [local(): lax.all_gather(factors[0], ('pair', 'aux'), axis=0, tiled=True)]
    all_gather x1 -> x0, waiting for transfers between devices: 18.9 us -> none  [local(): full_amp = lax.all_gather(amplitudes, 'aux', axis=1, tiled=True)]
    all_to_all x0 -> x1, starting transfers between devices: none -> 5.6 us  [local(): shards = lax.all_to_all(shards, 'aux', split_axis=0, concat_axis=0)]
    all_to_all x0 -> x1, local copies, waits for them, and re-layouts: none -> 5.56 us  [local(): shards = lax.all_to_all(shards, 'aux', split_axis=0, concat_axis=0)]
    all_to_all x1, waiting for transfers between devices: 59.4 us -> 64.6 us  [local(): incoming = lax.all_to_all(outgoing, 'pair', 0, 0, tiled=True)]
    another operation x0 -> x1, other arithmetic: none -> 4.58 us  [local(): shards = jnp.stack([amplitudes for _ in range(devices)])]
    all_to_all x0 -> x1, waiting for transfers between devices: none -> 4.46 us  [local(): shards = lax.all_to_all(shards, 'aux', split_axis=0, concat_axis=0)]
    convert_element_type x0 -> x1, local copies, waits for them, and re-layouts: none -> 2.85 us  [local(): outgoing = jnp.einsum('jp,pcb->jcb', owner_pick, rotated, preferred_eleme...]
  transfers between devices with their start and end apart: 4 -> 4, of which waited for: 4 -> 4; matrix products, arithmetic and copies ran while one was open for 10% -> 15% of each run, Pallas kernels for 0% -> 0%
where the time goes in v1:
time: 252 us; the launch traced here: 251 us
  waiting for transfers between devices  138 us (55%)
  matrix products  47.7 us (19%)
  starting transfers between devices  32.4 us (13%)
  local copies, waits for them, and re-layouts  14.4 us (6%)
  between operations  13.5 us (5%)
  other arithmetic  5.23 us (2%)
    all_to_all x1, waiting for transfers between devices, local(): incoming = lax.all_to_all(outgoing, 'pair', 0, 0, tiled=True)  64.6 us
    all_to_all x1, waiting for transfers between devices, local(): returned = lax.all_to_all(slot_back, 'pair', 0, 0, tiled=True)  50.2 us
    all_gather x1, waiting for transfers between devices, local(): lax.all_gather(factors[0], ('pair', 'aux'), axis=0, tiled=True)  18.1 us
    dot_general x1, matrix products, local(): jnp.einsum('pca,pba->pcb', own_cycle, margin, preferred_element_type=jnp....  15.8 us
    all_to_all x1, starting transfers between devices, local(): incoming = lax.all_to_all(outgoing, 'pair', 0, 0, tiled=True)  15 us
    dot_general x1, matrix products, local(): jnp.einsum('pac,pab->pcb', margin, halfway, preferred_element_type=jnp.fl...  14.1 us
    all_to_all x1, starting transfers between devices, local(): returned = lax.all_to_all(slot_back, 'pair', 0, 0, tiled=True)  11.8 us
    dot_general x1, matrix products, local(): jnp.dot(dressed, own_factors, preferred_element_type=jnp.float32)  11 us
  transfers between devices with their start and end apart: 4, of which 4 were waited for; matrix products, arithmetic and copies ran while one was open for 15% of the time, Pallas kernels for 0%

profile of v1, /device:TPU:32, one launch (start us, length us, event | category | flops | bytes accessed | tf_op | source)
XLA Modules:
  0.0 251.4 jit_solution(7913688990970154867)
XLA Ops:
  6.5 0.0 copy-start
  6.5 0.0 all-gather.3.cloned.1.call-start
  6.5 0.7 all-gather.3.cloned.1.call-update
  7.3 4.6 %pad_maximum_fusion = bf16[2,128,64,128]{3,2,1,0:T(8,128)(2,1)} fusion(bf16[1,128,64,128]{3,2,1,0:T(8,128)(2,1)} %bitcast.31), kind=kLoop, calls=%fused_computation.2 | loop fusion | flops 2097152 | bytes 6291456 | tf_op jit(solution)/shard_map/stack | solution.py:24
  11.8 5.6 %all-to-all-start = ((bf16[2,128,64,128]{3,2,1,0:T(8,128)(2,1)}), bf16[2,128,64,128]{3,2,1,0:T(8,128)(2,1)}, u32[]{:S(2)}, u32[]{:S(2)}) async-start(bf16[2,128,64,128]{3,2,1,0:T(8,128)(2,1)} %pad_maximum_fusion), calls=%async_computation | async-start | bytes 8388608 | tf_op jit(solution)/shard_map/all_to_all | solution.py:25
  17.5 0.0 copy-start.5
  17.5 4.5 %all-to-all-done = bf16[2,128,64,128]{3,2,1,0:T(8,128)(2,1)} async-done(((bf16[2,128,64,128]{3,2,1,0:T(8,128)(2,1)}), bf16[2,128,64,128]{3,2,1,0:T(8,128)(2,1)}, u32[]{:S(2)}, u32[]{:S(2)}) %all-to-all-start) | async-done | bytes 4194336 | tf_op jit(solution)/shard_map/all_to_all | solution.py:25
  21.9 5.6 %copy.23 = bf16[2,128,64,128]{3,2,0,1:T(8,128)(2,1)} copy(bf16[2,128,64,128]{3,2,1,0:T(8,128)(2,1)} %all-to-all-done) | data formatting | bytes 8388608 | tf_op jit(solution)/shard_map/all_to_all | solution.py:25
  27.5 0.0 copy-done
  27.5 0.0 copy-done.5
  27.5 3.2 %convolution_convert_fusion = bf16[128,128,128]{2,0,1:T(8,128)(2,1)} fusion(bf16[8,128,128]{2,1,0:T(8,128)(2,1)S(1)} %copy-done, s32[128]{0:T(128)S(1)} %copy-done.5), kind=kOutput, calls=%fused_computation.10 | convolution fusion | flops 35652608 | bytes 4456960 | tf_op jit(solution)/shard_map/po,oab->pab/dot_general | solution.py:30
  30.7 14.1 %fusion = bf16[128,128,128]{2,1,0:T(8,128)(2,1)} fusion(bf16[128,128,128]{2,1,0:T(8,128)(2,1)} %bitcast.30, bf16[128,128,128]{2,0,1:T(8,128)(2,1)} %convolution_convert_fusion), kind=kOutput, calls=%fused_computation.4 | convolution fusion | flops 1075838976 | bytes 12582912 | tf_op jit(solution)/shard_map/pac,pab->pcb/dot_general | solution.py:36
  44.9 0.0 copy-start.4
  44.9 1.8 dynamic-slice_convert_fusion
  46.7 0.0 copy-done.4
  46.7 1.8 fusion.13
  48.5 2.9 %copy.28 = bf16[128,64,128]{2,1,0:T(8,128)(2,1)} copy(bf16[128,64,128]{2,0,1:T(8,128)(2,1)S(1)} %fusion.13) | data formatting | bytes 4194304 | tf_op jit(solution)/shard_map/convert_element_type | solution.py:46
  51.3 15.0 %all-to-all-start.1 = ((bf16[128,64,128]{2,1,0:T(8,128)(2,1)}), bf16[128,64,128]{2,1,0:T(8,128)(2,1)S(1)}, u32[]{:S(2)}, u32[]{:S(2)}) async-start(bf16[128,64,128]{2,1,0:T(8,128)(2,1)} %copy.28), calls=%async_computation.1 | async-start | bytes 4194304 | tf_op jit(solution)/shard_map/all_to_all | solution.py:47
  66.3 64.6 %all-to-all-done.1 = bf16[128,64,128]{2,1,0:T(8,128)(2,1)S(1)} async-done(((bf16[128,64,128]{2,1,0:T(8,128)(2,1)}), bf16[128,64,128]{2,1,0:T(8,128)(2,1)S(1)}, u32[]{:S(2)}, u32[]{:S(2)}) %all-to-all-start.1) | async-done | bytes 2097184 | tf_op jit(solution)/shard_map/all_to_all | solution.py:47
  130.9 18.1 %all-gather.3.cloned.1.call-done = bf16[1,65536,128]{2,1,0:T(8,128)(2,1)} async-done(((bf16[1,256,128]{2,1,0:T(8,128)(2,1)}), bf16[1,65536,128]{2,1,0:T(8,128)(2,1)}) %all-gather.3.cloned.1.call-update) | async-done | bytes 16777232 | tf_op jit(solution)/shard_map/all_gather | solution.py:20
  149.0 11.0 %fusion.24 = bf16[64,128]{1,0:T(8,128)(2,1)S(1)} fusion(bf16[128,64,128]{2,1,0:T(8,128)(2,1)S(1)} %all-to-all-done.1, bf16[128,512,128]{2,1,0:T(8,128)(2,1)} %bitcast.29, s32[]{:T(128)S(6)} %select_n.14), kind=kOutput, calls=%fused_computation.21 | convolution fusion | flops 1082179584 | bytes 19021828 | tf_op jit(solution)/shard_map/dot_general | solution.py:51
  160.0 0.0 copy-start.1
  160.0 0.0 copy-start.3
  160.1 1.8 broadcast_in_dim.2
  161.9 11.8 %all-to-all-start.2 = ((bf16[128,64,128]{2,1,0:T(8,128)(2,1)}), bf16[128,64,128]{2,1,0:T(8,128)(2,1)S(1)}, u32[]{:S(2)}, u32[]{:S(2)}) async-start(bf16[128,64,128]{2,1,0:T(8,128)(2,1)} %broadcast_in_dim.2), calls=%async_computation.2 | async-start | bytes 4194304 | tf_op jit(solution)/shard_map/all_to_all | solution.py:54
  173.7 0.0 copy-done.1
  173.7 0.6 dynamic_slice.16
  174.4 1.2 gather_fusion
  175.6 0.0 copy-done.3
  175.6 0.1 constant_dynamic-slice_fusion
  175.7 0.6 broadcast_add_fusion
  176.4 50.2 %all-to-all-done.2 = bf16[128,64,128]{2,1,0:T(8,128)(2,1)S(1)} async-done(((bf16[128,64,128]{2,1,0:T(8,128)(2,1)}), bf16[128,64,128]{2,1,0:T(8,128)(2,1)S(1)}, u32[]{:S(2)}, u32[]{:S(2)}) %all-to-all-start.2) | async-done | bytes 2097184 | tf_op jit(solution)/shard_map/all_to_all | solution.py:54
  226.6 0.0 copy-start.2
  226.6 1.7 fusion.16
  228.3 0.4 copy-done.2
  228.7 15.8 %subtract_convert_fusion = bf16[128,64,128]{2,1,0:T(8,128)(2,1)} fusion(bf16[128,64,128]{2,1,0:T(8,128)(2,1)} %param.9, bf16[128,64,128]{2,1,0:T(8,128)(2,1)} %param.8, f32[128]{0:T(128)S(1)} %broadcast_add_fusion, f32[128,128]{1,0:T(8,128)S(1)} %copy-done.3, f32[128,64]{1,0:T(8,128)S(1)} %constant_dynamic-slice_fusion, ...), kind=kOutput, calls=%fused_computation.3 | convolution fusion | flops 276824064 | bytes 12681728 | tf_op jit(solution)/shard_map/pca,pba->pcb/dot_general | solution.py:58
  (2 shorter events, 0.0 us)
Async XLA Ops:
  6.5 21.0 %copy-start = (bf16[8,128,128]{2,1,0:T(8,128)(2,1)S(1)}, bf16[8,128,128]{2,1,0:T(8,128)(2,1)}, u32[]{:S(2)}) copy-start(bf16[8,128,128]{2,1,0:T(8,128)(2,1)} %param.10) | copy-start | bytes 786436
  6.5 142.5 %all-gather.3.cloned.1.call-start = ((), (), s32[]{:S(2)}) async-start(), calls=%async_computation.3 | async-start | bytes 16842752 | tf_op jit(solution)/shard_map/all_gather | solution.py:20
  11.8 10.1 %all-to-all-start = ((bf16[2,128,64,128]{3,2,1,0:T(8,128)(2,1)}), bf16[2,128,64,128]{3,2,1,0:T(8,128)(2,1)}, u32[]{:S(2)}, u32[]{:S(2)}) async-start(bf16[2,128,64,128]{3,2,1,0:T(8,128)(2,1)} %pad_maximum_fusion), calls=%async_computation | async-start | bytes 8388608 | tf_op jit(solution)/shard_map/all_to_all | solution.py:25
  17.5 10.0 %copy-start.5 = (s32[128]{0:T(128)S(1)}, s32[128]{0:T(128)}, u32[]{:S(2)}) copy-start(s32[128]{0:T(128)} %param.11) | copy-start | bytes 1540
  44.9 1.8 copy-start.4
  51.3 79.6 %all-to-all-start.1 = ((bf16[128,64,128]{2,1,0:T(8,128)(2,1)}), bf16[128,64,128]{2,1,0:T(8,128)(2,1)S(1)}, u32[]{:S(2)}, u32[]{:S(2)}) async-start(bf16[128,64,128]{2,1,0:T(8,128)(2,1)} %copy.28), calls=%async_computation.1 | async-start | bytes 4194304 | tf_op jit(solution)/shard_map/all_to_all | solution.py:47
  160.0 13.7 %copy-start.1 = (f32[128]{0:T(128)S(1)}, f32[128]{0:T(128)}, u32[]{:S(2)}) copy-start(f32[128]{0:T(128)} %param.14) | copy-start | bytes 1540
  160.0 15.6 %copy-start.3 = (f32[128,128]{1,0:T(8,128)S(1)}, f32[128,128]{1,0:T(8,128)}, u32[]{:S(2)}) copy-start(f32[128,128]{1,0:T(8,128)} %param.13) | copy-start | bytes 196612
  161.9 64.7 %all-to-all-start.2 = ((bf16[128,64,128]{2,1,0:T(8,128)(2,1)}), bf16[128,64,128]{2,1,0:T(8,128)(2,1)S(1)}, u32[]{:S(2)}, u32[]{:S(2)}) async-start(bf16[128,64,128]{2,1,0:T(8,128)(2,1)} %broadcast_in_dim.2), calls=%async_computation.2 | async-start | bytes 4194304 | tf_op jit(solution)/shard_map/all_to_all | solution.py:54
  226.6 2.2 copy-start.2
Sparse Core Ops, SparseCore 0:
  11.0 137.9 all-gather.2
